TPU v7x, 512 devices: a whole 4x8x8 slice. The times are simulated.
512 devices in a mesh: req: 128 (over z, y, core), grp: 4 (over x).
Axes of the slice: x: 4, y: 8, z: 8, core: 2. Of those that a mesh axis runs over, the one named last changes fastest.
Arguments:
- owner_slab: bfloat16 [65536, 1024], P('req'), may hold values from -6 to 6
- segment_ids: int32 [128, 512], P('req'), may hold values from 0 to 511, as said below
- head_weights: bfloat16 [1024, 16, 192], P(None, 'grp')
- merge_weights: bfloat16 [16, 64, 1024], P('grp'), may hold values from -0.1875 to 0.1875
- first_gain: float32 [1024], replicated, may hold values from 0.25 to 1.75
- first_bias: float32 [1024], replicated, may hold values from -3 to 3
- up_weights: bfloat16 [1024, 4096], P('req', 'grp'), may hold values from -0.1875 to 0.1875
- down_weights: bfloat16 [4096, 1024], P('grp', 'req'), may hold values from -0.09375 to 0.09375
- second_gain: float32 [1024], replicated, may hold values from 0.25 to 1.75
- second_bias: float32 [1024], replicated, may hold values from -3 to 3
- page_table: int32 [128, 4], P('req'), may hold values from 0 to 3, each once within a row
- row_map: int32 [128, 4, 128], P('req', 'grp'), may hold values from 0 to 127, each once within a row
Outputs:
- layer_out: bfloat16 [65536, 1024], P(('req', 'grp'))
- cache_pages: bfloat16 [512, 128, 16, 128], P('req', None, 'grp')
Inputs may be any that keep to these rules, and one draw needn't show every extreme that they name: `segment_ids`: within each slab the ids start at 0, never fall and rise by at most one from row to row; in one slab all 512 rows form a single request, and in one other slab every row is a request of its own.
All inputs are finite; a program needn't handle non-finite values.
Results may differ from a plain program's by a relative error of at most 0.0075.
Values may be sent and summed in bfloat16 or wider, within the bound.
No kernel may reach another device: no remote copies, remote signals or barrier semaphores. Data moves between devices by JAX's collectives and lax.ppermute only.
A program may use at most 64 MiB of HBM per device.

v0:
```python
import math
import jax
import jax.numpy as jnp
from jax import lax
from jax.sharding import PartitionSpec as P

EPSILON = 1e-05


def layer_norm(values, gain, bias):
    center = values - jnp.mean(values, axis=-1, keepdims=True)
    spread = jnp.mean(center * center, axis=-1, keepdims=True)
    return center * lax.rsqrt(spread + EPSILON) * gain + bias


def local(
    owner_slab,
    segment_ids,
    head_weights,
    merge_weights,
    first_gain,
    first_bias,
    up_weights,
    down_weights,
    second_gain,
    second_bias,
    page_table,
    row_map,
):
    group = lax.axis_size("grp")
    owners = lax.axis_size("req")
    rows_all = owner_slab.shape[0]
    width = owner_slab.shape[1]
    quarter = rows_all // group
    local_heads = head_weights.shape[1]
    head_dim = head_weights.shape[2] // 3
    projected = jnp.einsum(
        "nd,dhc->nhc", owner_slab, head_weights, preferred_element_type=jnp.float32
    ).astype(jnp.bfloat16)
    queries = jnp.moveaxis(projected[:, :, :head_dim], 1, 0)
    key_rows = jnp.moveaxis(projected[:, :, head_dim : 2 * head_dim], 1, 0)
    value_rows = jnp.moveaxis(projected[:, :, 2 * head_dim :], 1, 0)
    segment = segment_ids[0]
    position = jnp.arange(rows_all, dtype=jnp.int32)
    allowed = (position[:, None] >= position[None, :]) & (segment[:, None] == segment[None, :])
    scale = 1.0 / math.sqrt(head_dim)

    def one_head(operands):
        query_head, key_head, value_head = operands
        scores = (
            lax.dot_general(
                query_head, key_head, (((1,), (1,)), ((), ())), preferred_element_type=jnp.float32
            )
            * scale
        )
        scores = jnp.where(allowed, scores, -1e30)
        probs = jax.nn.softmax(scores, axis=-1).astype(jnp.bfloat16)
        return jnp.dot(probs, value_head, preferred_element_type=jnp.float32).astype(jnp.bfloat16)

    attended = jnp.moveaxis(lax.map(one_head, (queries, key_rows, value_rows)), 0, 1)
    own = lax.axis_index("grp")
    own_rows = lax.dynamic_slice_in_dim(owner_slab, own * quarter, quarter, 0).astype(jnp.float32)
    partial_rows = jnp.einsum(
        "nhd,hde->ne", attended, merge_weights, preferred_element_type=jnp.float32
    )
    mixed = lax.psum_scatter(partial_rows, "grp", scatter_dimension=0, tiled=True)
    hidden = layer_norm(own_rows + mixed, first_gain, first_bias).astype(jnp.bfloat16)
    slots = quarter // owners
    placed = jnp.zeros_like(hidden).at[row_map[0, 0]].set(hidden)
    arrived = lax.all_to_all(
        placed.reshape(owners, slots, width), "req", split_axis=0, concat_axis=0, tiled=True
    )
    even_rows = arrived.reshape(quarter, width)
    group_rows = lax.all_gather(even_rows, "grp", axis=0, tiled=True)
    raised = jnp.dot(
        group_rows,
        lax.all_gather(up_weights, "req", axis=0, tiled=True),
        preferred_element_type=jnp.float32,
    )
    activated = jax.nn.gelu(raised, approximate=False).astype(jnp.bfloat16)
    lowered_all = jnp.dot(
        activated,
        lax.all_gather(down_weights, "req", axis=1, tiled=True),
        preferred_element_type=jnp.float32,
    )
    lowered = lax.psum_scatter(lowered_all, "grp", scatter_dimension=0, tiled=True)
    layer_out = layer_norm(
        even_rows.astype(jnp.float32) + lowered, second_gain, second_bias
    ).astype(jnp.bfloat16)
    page_count = page_table.shape[1]
    page_rows = rows_all // page_count
    stacked = projected[:, :, head_dim:].reshape(page_count, page_rows, local_heads, 2 * head_dim)
    cache_pages = jnp.zeros_like(stacked).at[page_table[0]].set(stacked)
    return (layer_out, cache_pages)


def solution(mesh):
    in_specs = (
        P("req", None),
        P("req", None),
        P(None, "grp", None),
        P("grp", None, None),
        P(),
        P(),
        P("req", "grp"),
        P("grp", "req"),
        P(),
        P(),
        P("req", None),
        P("req", "grp", None),
    )
    out_specs = (P(("req", "grp"), None), P("req", None, "grp", None))
    return jax.shard_map(local, mesh=mesh, in_specs=in_specs, out_specs=out_specs, check_vma=False)
```

profile of v0, /device:TPU:1, one launch (start us, length us, event | category | flops | bytes accessed | tf_op | source)
XLA Modules:
  0.0 281.3 jit_solution(15280526608803334837)
XLA Ops:
  8.1 1.3 copy-done
  9.4 2.2 fusion.105
  11.7 0.1 convert_element_type.25
  11.8 0.1 slice_bitcast_fusion
  11.9 0.5 copy-done.7
  12.3 3.7 %while.11 = (s32[]{:T(128)}, bf16[4,512,64]{1,2,0:T(8,128)(2,1)S(1)}, bf16[4,512,64]{1,2,0:T(8,128)(2,1)S(1)}, bf16[4,512,64]{1,2,0:T(8,128)(2,1)S(1)}, bf16[4,5...) while((s32[]{:T(128)}, bf16[4,512,64]{1,2,0:T(8,128)(2,1)S(1)}, ...), condition=%wide.region_3.4_spmd.clone, body=%wide.region_0.3_spmd.clone.sunk | while | flops 70024192 | bytes 3424341 | solution.py:60
  12.3 0.4 fusion.116
  12.7 0.2 fusion.117
  12.9 0.3 fusion.118
  13.3 0.4 fusion.116
  13.7 0.2 fusion.117
  13.9 0.3 fusion.118
  14.2 0.4 fusion.116
  14.6 0.2 fusion.117
  14.8 0.3 fusion.118
  15.1 0.4 fusion.116
  15.6 0.2 fusion.117
  15.8 0.3 fusion.118
  16.1 0.7 copy-done.10
  16.8 3.0 %convolution_bitcast_fusion = f32[512,1024]{1,0:T(8,128)} fusion(bf16[4,64,1024]{2,1,0:T(8,128)(2,1)} %param.17, bf16[4,512,64]{1,2,0:T(8,128)(2,1)} %copy-done.10), kind=kOutput, calls=%fused_computation.40 | convolution fusion | flops 268435456 | bytes 2883584 | tf_op jit(solution)/shard_map/nhd,hde->ne/dot_general | solution.py:63
  19.8 0.0 all-gather.5.cloned.1.call-start
  19.9 0.5 all-gather.5.cloned.1.call-update
  20.4 0.5 all-gather.7.cloned.1.call-update
  21.1 39.4 %reduce-scatter.3.cloned.1.call-done = f32[128,1024]{1,0:T(8,128)} async-done(((f32[512,1024]{1,0:T(8,128)}), f32[128,1024]{1,0:T(8,128)}) %reduce-scatter.3.cloned.1.call-update) | async-done | bytes 524304 | tf_op jit(solution)/shard_map/reduce_scatter | solution.py:66
  60.4 1.2 fusion.70
  61.6 1.2 multiply_reduce_fusion.1
  62.9 1.9 scatter_custom_fusion
  64.8 0.5 broadcast.106
  65.3 0.8 reduce
  66.1 0.2 reshape.126
  66.3 30.1 %all_to_all.5 = bf16[128,2,512]{2,1,0:T(2,128)(2,1)S(1)} all-to-all(bf16[128,2,512]{2,1,0:T(2,128)(2,1)S(1)} %reshape.126), channel_id=1, replica_groups=mesh['req'=128,'grp'=4] {'req'}, dimensions={0} | all-to-all | bytes 524288 | tf_op jit(solution)/shard_map/all_to_all | solution.py:70
  96.4 0.2 reshape.127
  96.6 0.8 copy.29
  97.4 0.2 reduce-scatter.5.cloned.1.call-start
  97.7 16.5 %all-gather.5.cloned.1.call-done = bf16[1024,1024]{1,0:T(8,128)(2,1)} async-done(((bf16[8,1024]{1,0:T(8,128)(2,1)}), bf16[1024,1024]{1,0:T(8,128)(2,1)}) %all-gather.5.cloned.1.call-update) | async-done | bytes 2097168 | tf_op jit(solution)/shard_map/all_gather | solution.py:77
  114.2 82.0 %all-gather.7.cloned.1.call-done = bf16[1024,1024]{0,1:T(8,128)(2,1)} async-done(((bf16[1024,8]{0,1:T(8,128)(2,1)}), bf16[1024,1024]{0,1:T(8,128)(2,1)}) %all-gather.7.cloned.1.call-update) | async-done | bytes 2097168 | tf_op jit(solution)/shard_map/all_gather | solution.py:83
  196.1 26.4 %all-gather.9.cloned.1.call-done = bf16[512,1,1024]{2,0,1:T(8,128)(2,1)} async-done(((bf16[128,1,1024]{2,0,1:T(8,128)(2,1)}), bf16[512,1,1024]{2,0,1:T(8,128)(2,1)}) %all-gather.9.cloned.1.call-update) | async-done | bytes 1048592 | tf_op jit(solution)/shard_map/all_gather | solution.py:74
  222.5 10.1 %fusion.25 = f32[512,1024]{1,0:T(8,128)} fusion(bf16[1024,1024]{0,1:T(8,128)(2,1)} %all-gather.7.cloned.1.call-done, bf16[1024,1024]{1,0:T(8,128)(2,1)} %all-gather.5.cloned.1.call-done, bf16[512,1,1024]{2,0,1:T(8,128)(2,1)} %all-gather.9.cloned.1.call-done), kind=kOutput, calls=%fused_computation.41 | convolution fusion | flops 2181562368 | bytes 7340032 | tf_op jit(solution)/shard_map/dot_general | solution.py:81
  232.7 0.1 reshape.115
  232.8 0.4 copy.31
  233.2 0.1 copy-done.9
  233.3 0.1 broadcast_in_dim.18
  233.4 0.8 scatter_fusion
  234.2 1.2 copy.32
  235.4 34.8 %reduce-scatter.5.cloned.1.call-done = f32[128,1024]{1,0:T(8,128)} async-done(((f32[512,1024]{1,0:T(8,128)}), f32[128,1024]{1,0:T(8,128)}) %reduce-scatter.5.cloned.1.call-update) | async-done | bytes 524304 | tf_op jit(solution)/shard_map/reduce_scatter | solution.py:86
  270.2 1.3 fusion.69
  271.5 1.3 multiply_reduce_fusion
  272.8 0.9 add_convert_fusion
  (32 shorter events, 0.3 us)
Async XLA Ops:
  8.0 1.4 copy-start
  8.0 52.4 %reduce-scatter.3.cloned.1.call-start = ((), (), s32[]{:S(2)}) async-start(), calls=%async_computation.3 | async-start | bytes 2621440 | tf_op jit(solution)/shard_map/reduce_scatter | solution.py:66
  11.6 0.7 copy-start.7
  16.1 0.7 copy-start.10
  16.8 4.3 %copy-start.8 = (s32[1,1,128]{2,1,0:T(1,128)S(1)}, s32[1,1,128]{2,1,0:T(1,128)}, u32[]{:S(2)}) copy-start(s32[1,1,128]{2,1,0:T(1,128)} %param.25) | copy-start | bytes 1540
  16.8 43.6 %copy-start.2 = (bf16[512,1024]{1,0:T(8,128)(2,1)S(1)}, bf16[512,1024]{1,0:T(8,128)(2,1)}, u32[]{:S(2)}) copy-start(bf16[512,1024]{1,0:T(8,128)(2,1)} %param.14) | copy-start | bytes 3145732
  19.8 43.1 %copy-start.3 = (f32[1024]{0:T(1024)S(1)}, f32[1024]{0:T(1024)}, u32[]{:S(2)}) copy-start(f32[1024]{0:T(1024)} %param.19) | copy-start | bytes 12292
  19.8 43.1 %copy-start.4 = (f32[1024]{0:T(1024)S(1)}, f32[1024]{0:T(1024)}, u32[]{:S(2)}) copy-start(f32[1024]{0:T(1024)} %param.18) | copy-start | bytes 12292
  19.8 94.3 %all-gather.5.cloned.1.call-start = ((), (), s32[]{:S(2)}) async-start(), calls=%async_computation.4 | async-start | bytes 2113536 | tf_op jit(solution)/shard_map/all_gather | solution.py:77
  20.4 175.7 %all-gather.7.cloned.1.call-start = ((), (), s32[]{:S(2)}) async-start(), calls=%async_computation.5 | async-start | bytes 2113536 | tf_op jit(solution)/shard_map/all_gather | solution.py:83
  21.0 201.5 %all-gather.9.cloned.1.call-start = ((), (), s32[]{:S(2)}) async-start(), calls=%async_computation.7 | async-start | bytes 1310720 | tf_op jit(solution)/shard_map/all_gather | solution.py:74
  97.4 172.8 %reduce-scatter.5.cloned.1.call-start = ((), (), s32[]{:S(2)}) async-start(), calls=%async_computation.6 | async-start | bytes 2621440 | tf_op jit(solution)/shard_map/reduce_scatter | solution.py:86
  232.6 0.7 copy-start.9
  233.4 39.4 %copy-start.5 = (f32[1024]{0:T(1024)S(1)}, f32[1024]{0:T(1024)}, u32[]{:S(2)}) copy-start(f32[1024]{0:T(1024)} %param.23) | copy-start | bytes 12292
  233.4 39.4 %copy-start.6 = (f32[1024]{0:T(1024)S(1)}, f32[1024]{0:T(1024)}, u32[]{:S(2)}) copy-start(f32[1024]{0:T(1024)} %param.22) | copy-start | bytes 12292
  270.2 2.6 copy-start.1
Sparse Core Ops, SparseCore 0:
  19.9 40.4 reduce-scatter.2
  232.8 37.4 reduce-scatter.4
Sparse Core Ops, SparseCore 1:
  23.4 90.7 all-gather.4
  117.2 78.9 all-gather.6
  198.7 23.8 all-gather.8
where the time goes:
time: 282 us; the launch traced here: 281 us
  waiting for transfers between devices  200 us (71%)
  blocking collectives  30.1 us (11%)
  matrix products  18.2 us (6%)
  between operations  15.9 us (6%)
  other arithmetic  9.46 us (3%)
  local copies, waits for them, and re-layouts  7.03 us (2%)
    all_gather x1, waiting for transfers between devices, local(): lax.all_gather(down_weights, 'req', axis=1, tiled=True)  82 us
    reduce_scatter x1, waiting for transfers between devices, local(): lax.psum_scatter(partial_rows, 'grp', scatter_dimension=0, tiled=True)  39.4 us
    reduce_scatter x1, waiting for transfers between devices, local(): lax.psum_scatter(lowered_all, 'grp', scatter_dimension=0, tiled=True)  34.8 us
    all_to_all x1, blocking collectives, local(): lax.all_to_all(placed.reshape(owners, slots, width), 'req', split_axis=0,...  30.1 us
    all_gather x1, waiting for transfers between devices, local(): group_rows = lax.all_gather(even_rows, 'grp', axis=0, tiled=True)  26.4 us
    all_gather x1, waiting for transfers between devices, local(): lax.all_gather(up_weights, 'req', axis=0, tiled=True)  16.5 us
    dot_general x1, matrix products, local(): jnp.dot(activated, lax.all_gather(down_weights, 'req', axis=1, tiled=True...  10.1 us
  transfers between devices with their start and end apart: 5, of which 5 were waited for; matrix products, arithmetic and copies ran while one was open for 3% of the time, Pallas kernels for 0%

commit v1 on v0

--- a/solution.py
+++ b/solution.py
@@ -71,7 +71,19 @@
         placed.reshape(owners, slots, width), "req", split_axis=0, concat_axis=0, tiled=True
     )
     even_rows = arrived.reshape(quarter, width)
-    group_rows = lax.all_gather(even_rows, "grp", axis=0, tiled=True)
+    dev_n = lax.psum(1, "grp")
+    store = [(d, (d + 1) % dev_n) for d in range(dev_n)]
+    queue = [(d, (d - 1) % dev_n) for d in range(dev_n)]
+    block_next, found_now = ([even_rows], [even_rows])
+    for _ in range(dev_n // 2):
+        block_next.append(lax.ppermute(block_next[-1], "grp", store))
+    for _ in tuple(range((dev_n - 1) // 2)):
+        found_now.append(lax.ppermute(found_now[-1], "grp", queue))
+    group_rows = jnp.roll(
+        jnp.concatenate([*block_next[::-1], *found_now[1:]], 0),
+        (lax.axis_index("grp") - dev_n // 2) * even_rows.shape[0],
+        0,
+    )
     raised = jnp.dot(
         group_rows,
         lax.all_gather(up_weights, "req", axis=0, tiled=True),

time: 282 us -> 249 us (0.88)
  waiting for transfers between devices: 200 us -> 153 us
  starting transfers between devices: 0.38 us -> 8.73 us
  local copies, waits for them, and re-layouts: 7.03 us -> 13 us
    all_gather x1 -> x0, waiting for transfers between devices: 26.4 us -> none  [local(): group_rows = lax.all_gather(even_rows, 'grp', axis=0, tiled=True)]
    all_gather x1, waiting for transfers between devices: 16.5 us -> 0.01 us  [local(): lax.all_gather(up_weights, 'req', axis=0, tiled=True)]
    ppermute x0 -> x3, waiting for transfers between devices: none -> 11.9 us  [the longest x2 11.9 us: local(): block_next.append(lax.ppermute(block_next[-1], 'grp', store))]
    all_gather x1, waiting for transfers between devices: 82 us -> 72.3 us  [local(): lax.all_gather(down_weights, 'req', axis=1, tiled=True)]
    ppermute x0 -> x3, starting transfers between devices: none -> 8.57 us  [the longest x1 4.75 us: local(): found_now.append(lax.ppermute(found_now[-1], 'grp', queue))]
    unnamed x25 -> x33, local copies, waits for them, and re-layouts: 4.26 us -> 10.2 us
    reduce_scatter x1, waiting for transfers between devices: 34.8 us -> 28.9 us  [local(): lax.psum_scatter(lowered_all, 'grp', scatter_dimension=0, tiled=True)]
  transfers between devices with their start and end apart: 5 -> 7, of which waited for: 5 -> 5; matrix products, arithmetic and copies ran while one was open for 3% -> 6% of each run, Pallas kernels for 0% -> 0%
where the time goes in v1:
time: 249 us
  waiting for transfers between devices  153 us (61%)
  blocking collectives  30.1 us (12%)
  matrix products  18.2 us (7%)
  between operations  15.8 us (6%)
  local copies, waits for them, and re-layouts  13 us (5%)
  other arithmetic  9.46 us (4%)
  starting transfers between devices  8.73 us (4%)
    all_gather x1, waiting for transfers between devices, local(): lax.all_gather(down_weights, 'req', axis=1, tiled=True)  72.3 us
    reduce_scatter x1, waiting for transfers between devices, local(): lax.psum_scatter(partial_rows, 'grp', scatter_dimension=0, tiled=True)  39.3 us
    all_to_all x1, blocking collectives, local(): lax.all_to_all(placed.reshape(owners, slots, width), 'req', split_axis=0,...  30.1 us
    reduce_scatter x1, waiting for transfers between devices, local(): lax.psum_scatter(lowered_all, 'grp', scatter_dimension=0, tiled=True)  28.9 us
    ppermute x2, waiting for transfers between devices, local(): block_next.append(lax.ppermute(block_next[-1], 'grp', store))  11.9 us
    unnamed x33, local copies, waits for them, and re-layouts  10.2 us
    dot_general x1, matrix products, local(): jnp.dot(activated, lax.all_gather(down_weights, 'req', axis=1, tiled=True...  10.1 us
  transfers between devices with their start and end apart: 7, of which 5 were waited for; matrix products, arithmetic and copies ran while one was open for 6% of the time, Pallas kernels for 0%

profile of v1, /device:TPU:1, one launch (start us, length us, event | category | flops | bytes accessed | tf_op | source)
XLA Modules:
  0.0 248.8 jit_solution(7250108298290878919)
XLA Ops:
  8.1 1.3 copy-done
  9.4 2.2 fusion.107
  11.9 0.5 copy-done.7
  12.3 3.7 %while.11 = (s32[]{:T(128)}, bf16[4,512,64]{1,2,0:T(8,128)(2,1)S(1)}, bf16[4,512,64]{1,2,0:T(8,128)(2,1)S(1)}, bf16[4,512,64]{1,2,0:T(8,128)(2,1)S(1)}, bf16[4,5...) while((s32[]{:T(128)}, bf16[4,512,64]{1,2,0:T(8,128)(2,1)S(1)}, ...), condition=%wide.region_3.4_spmd.clone, body=%wide.region_0.3_spmd.clone.sunk | while | flops 70024192 | bytes 3424333 | solution.py:60
  12.3 0.4 fusion.118
  12.7 0.2 fusion.119
  12.9 0.3 fusion.120
  13.3 0.4 fusion.118
  13.9 0.3 fusion.120
  14.2 0.4 fusion.118
  14.8 0.3 fusion.120
  15.1 0.4 fusion.118
  15.8 0.3 fusion.120
  16.1 0.7 copy-done.10
  16.8 3.0 %convolution_bitcast_fusion = f32[512,1024]{1,0:T(8,128)} fusion(bf16[4,64,1024]{2,1,0:T(8,128)(2,1)} %param.17, bf16[4,512,64]{1,2,0:T(8,128)(2,1)} %copy-done.10), kind=kOutput, calls=%fused_computation.40 | convolution fusion | flops 268435456 | bytes 2883584 | tf_op jit(solution)/shard_map/nhd,hde->ne/dot_general | solution.py:63
  19.9 0.5 all-gather.3.cloned.1.call-update
  20.4 0.5 all-gather.5.cloned.1.call-update
  21.1 39.3 %reduce-scatter.3.cloned.1.call-done = f32[128,1024]{1,0:T(8,128)} async-done(((f32[512,1024]{1,0:T(8,128)}), f32[128,1024]{1,0:T(8,128)}) %reduce-scatter.3.cloned.1.call-update) | async-done | bytes 524304 | tf_op jit(solution)/shard_map/reduce_scatter | solution.py:66
  60.4 1.2 fusion.70
  61.6 1.2 multiply_reduce_fusion.1
  62.9 1.9 scatter_custom_fusion
  64.8 0.5 broadcast.107
  65.3 0.8 reduce
  66.3 30.1 %all_to_all.5 = bf16[128,2,512]{2,1,0:T(2,128)(2,1)S(1)} all-to-all(bf16[128,2,512]{2,1,0:T(2,128)(2,1)S(1)} %reshape.124), channel_id=1, replica_groups=mesh['req'=128,'grp'=4] {'req'}, dimensions={0} | all-to-all | bytes 524288 | tf_op jit(solution)/shard_map/all_to_all | solution.py:70
  96.4 0.2 reshape.125
  96.6 0.8 copy.45
  97.4 1.9 collective-permute-start
  99.3 8.9 %collective-permute-done = bf16[128,1024]{1,0:T(8,128)(2,1)S(1)} collective-permute-done((bf16[128,1024]{1,0:T(8,128)(2,1)}, bf16[128,1024]{1,0:T(8,128)(2,1)S(1)}, u32[]{:S(2)}, u32[]{:S(2)}) %collective-permute-start) | collective-permute-done | bytes 262176 | tf_op jit(solution)/shard_map/ppermute | solution.py:79
  108.2 1.9 collective-permute-start.1
  110.1 4.8 %collective-permute-start.2 = (bf16[128,1024]{1,0:T(8,128)(2,1)}, bf16[128,1024]{1,0:T(8,128)(2,1)S(1)}, u32[]{:S(2)}, u32[]{:S(2)}) collective-permute-start(bf16[128,1024]{1,0:T(8,128)(2,1)} %bitcast.62), channel_id=1, source_target_pairs={{0,3},{1,0},{2,1},{3,2},{4,7},{5,4},{6,5},{7,6},{8,11},{9,8},{10,9... | collective-permute-start | bytes 786440 | tf_op jit(solution)/shard_map/ppermute | solution.py:81
  114.9 3.0 %collective-permute-done.1 = bf16[128,1024]{1,0:T(8,128)(2,1)S(1)} collective-permute-done((bf16[128,1024]{1,0:T(8,128)(2,1)S(1)}, bf16[128,1024]{1,0:T(8,128)(2,1)S(1)}, u32[]{:S(2)}, u32[]{:S(2)}) %collective-permute-start.1) | collective-permute-done | bytes 262176 | tf_op jit(solution)/shard_map/ppermute | solution.py:79
  117.9 0.7 constant_dynamic-update-slice_fusion.7
  118.6 0.7 constant_dynamic-update-slice_fusion.6
  119.3 0.8 constant_dynamic-update-slice_fusion.5
  120.1 0.7 constant_dynamic-update-slice_fusion.4
  120.9 0.7 constant_dynamic-update-slice_fusion.3
  121.6 0.7 constant_dynamic-update-slice_fusion.2
  122.3 0.8 constant_dynamic-update-slice_fusion.1
  123.1 0.7 constant_dynamic-update-slice_fusion
  123.8 72.3 %all-gather.5.cloned.1.call-done = bf16[1024,1024]{0,1:T(8,128)(2,1)} async-done(((bf16[1024,8]{0,1:T(8,128)(2,1)}), bf16[1024,1024]{0,1:T(8,128)(2,1)}) %all-gather.5.cloned.1.call-update) | async-done | bytes 2097168 | tf_op jit(solution)/shard_map/all_gather | solution.py:95
  196.1 10.1 %fusion.25 = f32[512,1024]{1,0:T(8,128)} fusion(bf16[1024,1024]{0,1:T(8,128)(2,1)} %all-gather.5.cloned.1.call-done, bf16[1024,1024]{1,0:T(8,128)(2,1)} %all-gather.3.cloned.1.call-done, bf16[1024,1024]{1,0:T(8,128)(2,1)} %constant_dynamic-update-slice_fusion, s32[]{:T(128)S(6)} %select_n.43), kind=kOutput, calls=%fused_computation.41 | convolution fusion | flops 2181562368 | bytes 7340036 | tf_op jit(solution)/shard_map/dot_general | solution.py:93
  206.4 0.4 copy.28
  207.0 0.8 scatter_fusion
  207.8 1.2 copy.29
  209.0 28.9 %reduce-scatter.5.cloned.1.call-done = f32[128,1024]{1,0:T(8,128)} async-done(((f32[512,1024]{1,0:T(8,128)}), f32[128,1024]{1,0:T(8,128)}) %reduce-scatter.5.cloned.1.call-update) | async-done | bytes 524304 | tf_op jit(solution)/shard_map/reduce_scatter | solution.py:98
  237.9 1.3 fusion.69
  239.2 1.3 multiply_reduce_fusion
  240.5 0.9 add_convert_fusion
  (43 shorter events, 1.6 us)
Async XLA Ops:
  8.0 1.4 copy-start
  8.0 52.4 %reduce-scatter.3.cloned.1.call-start = ((), (), s32[]{:S(2)}) async-start(), calls=%async_computation.3 | async-start | bytes 2621440 | tf_op jit(solution)/shard_map/reduce_scatter | solution.py:66
  11.6 0.7 copy-start.7
  16.1 0.7 copy-start.10
  16.8 4.3 %copy-start.8 = (s32[1,1,128]{2,1,0:T(1,128)S(1)}, s32[1,1,128]{2,1,0:T(1,128)}, u32[]{:S(2)}) copy-start(s32[1,1,128]{2,1,0:T(1,128)} %param.25) | copy-start | bytes 1540
  16.8 43.6 %copy-start.2 = (bf16[512,1024]{1,0:T(8,128)(2,1)S(1)}, bf16[512,1024]{1,0:T(8,128)(2,1)}, u32[]{:S(2)}) copy-start(bf16[512,1024]{1,0:T(8,128)(2,1)} %param.14) | copy-start | bytes 3145732
  19.8 43.1 %copy-start.3 = (f32[1024]{0:T(1024)S(1)}, f32[1024]{0:T(1024)}, u32[]{:S(2)}) copy-start(f32[1024]{0:T(1024)} %param.19) | copy-start | bytes 12292
  19.8 43.1 %copy-start.4 = (f32[1024]{0:T(1024)S(1)}, f32[1024]{0:T(1024)}, u32[]{:S(2)}) copy-start(f32[1024]{0:T(1024)} %param.18) | copy-start | bytes 12292
  19.8 104.0 %all-gather.3.cloned.1.call-start = ((), (), s32[]{:S(2)}) async-start(), calls=%async_computation.4 | async-start | bytes 2113536 | tf_op jit(solution)/shard_map/all_gather | solution.py:89
  20.4 175.7 %all-gather.5.cloned.1.call-start = ((), (), s32[]{:S(2)}) async-start(), calls=%async_computation.5 | async-start | bytes 2113536 | tf_op jit(solution)/shard_map/all_gather | solution.py:95
  21.0 216.9 %reduce-scatter.5.cloned.1.call-start = ((), (), s32[]{:S(2)}) async-start(), calls=%async_computation.6 | async-start | bytes 2621440 | tf_op jit(solution)/shard_map/reduce_scatter | solution.py:98
  97.4 10.8 %collective-permute-start = (bf16[128,1024]{1,0:T(8,128)(2,1)}, bf16[128,1024]{1,0:T(8,128)(2,1)S(1)}, u32[]{:S(2)}, u32[]{:S(2)}) collective-permute-start(bf16[128,1024]{1,0:T(8,128)(2,1)} %bitcast.62), channel_id=1, source_target_pairs={{0,1},{1,2},{2,3},{3,0},{4,5},{5,6},{6,7},{7,4},{8,9},{9,10},{10,1... | collective-permute-start | bytes 786440 | tf_op jit(solution)/shard_map/ppermute | solution.py:79
  108.2 9.7 %collective-permute-start.1 = (bf16[128,1024]{1,0:T(8,128)(2,1)S(1)}, bf16[128,1024]{1,0:T(8,128)(2,1)S(1)}, u32[]{:S(2)}, u32[]{:S(2)}) collective-permute-start(bf16[128,1024]{1,0:T(8,128)(2,1)S(1)} %collective-permute-done), channel_id=1, source_target_pairs={{0,1},{1,2},{2,3},{3,0},{4,5},{5,6},{6,7},{7,4},{8,9},{9,10},{10,1... | collective-permute-start | bytes 786440 | tf_op jit(solution)/shard_map/ppermute | solution.py:79
  110.1 10.0 %collective-permute-start.2 = (bf16[128,1024]{1,0:T(8,128)(2,1)}, bf16[128,1024]{1,0:T(8,128)(2,1)S(1)}, u32[]{:S(2)}, u32[]{:S(2)}) collective-permute-start(bf16[128,1024]{1,0:T(8,128)(2,1)} %bitcast.62), channel_id=1, source_target_pairs={{0,3},{1,0},{2,1},{3,2},{4,7},{5,4},{6,5},{7,6},{8,11},{9,8},{10,9... | collective-permute-start | bytes 786440 | tf_op jit(solution)/shard_map/ppermute | solution.py:81
  206.3 0.7 copy-start.9
  207.0 33.4 %copy-start.5 = (f32[1024]{0:T(1024)S(1)}, f32[1024]{0:T(1024)}, u32[]{:S(2)}) copy-start(f32[1024]{0:T(1024)} %param.23) | copy-start | bytes 12292
  207.0 33.4 %copy-start.6 = (f32[1024]{0:T(1024)S(1)}, f32[1024]{0:T(1024)}, u32[]{:S(2)}) copy-start(f32[1024]{0:T(1024)} %param.22) | copy-start | bytes 12292
  237.9 2.6 %copy-start.1 = (f32[128,1024]{1,0:T(8,128)S(1)}, f32[128,1024]{1,0:T(8,128)}, u32[]{:S(2)}) copy-start(f32[128,1024]{1,0:T(8,128)} %reduce-scatter.5.cloned.1.call-done) | copy-start | bytes 1572868
Sparse Core Ops, SparseCore 0:
  19.9 40.4 reduce-scatter.2
  206.4 31.4 reduce-scatter.4
Sparse Core Ops, SparseCore 1:
  23.4 90.7 all-gather.2
  117.2 78.9 all-gather.4
